TPU v7x, 256 devices: a whole 4x4x8 slice. The times are simulated.
256 devices in a mesh: grp: 32 (over x, z), shard: 8 (over y, core).
Axes of the slice: x: 4, y: 4, z: 8, core: 2. Of those that a mesh axis runs over, the one named last changes fastest.
Arguments:
- layer_inputs: bfloat16 [131072, 1600], P(('grp', 'shard')), may hold values from -6 to 6
- cotangents: bfloat16 [131072, 1600], P(('grp', 'shard')), may hold values from -0.25 to 0.25
- weight: bfloat16 [1600, 1600], P('shard'), may hold values from -0.15625 to 0.15625
- error_state: float32 [32, 1600, 1600], P('grp', 'shard'), may hold values from -6 to 6
- momentum: float32 [1600, 1600], P('shard'), may hold values from -0.75 to 0.75
- bias_momentum: float32 [1600], replicated, may hold values from -6 to 6
- start_basis: float32 [1600, 32], replicated, may hold values from -6 to 6
- next_inputs: bfloat16 [131072, 1600], P(('grp', 'shard')), may hold values from -6 to 6
Outputs:
- next_outputs: bfloat16 [131072, 1600], P(('grp', 'shard'))
- new_error: float32 [32, 1600, 1600], P('grp', 'shard')
- new_momentum: float32 [1600, 1600], P('shard')
- new_bias_momentum: float32 [1600], replicated
All inputs are finite; a program needn't handle non-finite values.
Results may differ from a plain program's by a relative error of at most 0.015.
Values may be sent and summed in bfloat16 or wider, within the bound.
No kernel may reach another device: no remote copies, remote signals or barrier semaphores. Data moves between devices by JAX's collectives and lax.ppermute only.
A program may use at most 128 MiB of HBM per device.

v0:
```python
import jax
import jax.numpy as jnp
from jax import lax
from jax.sharding import PartitionSpec as P

momentum_decay = 0.9
learn_rate = 0.1


def shards(
    layer_inputs, cotangents, weight, error_state, momentum, bias_momentum, start_basis, next_inputs
):
    highest = lax.Precision.HIGHEST
    group_count = lax.axis_size("grp")
    rank = start_basis.shape[1]
    gradient = lax.psum_scatter(
        lax.dot_general(
            layer_inputs, cotangents, (((0,), (0,)), ((), ())), preferred_element_type=jnp.float32
        ).astype(jnp.bfloat16),
        "shard",
        scatter_dimension=0,
        tiled=True,
    ).astype(jnp.float32)
    column_sums = jnp.sum(cotangents, axis=0, dtype=jnp.float32)
    corrected = gradient + error_state[0]
    summed = lax.psum(jnp.concatenate([corrected, column_sums[None, :]], axis=0), "grp")
    total = summed[:-1]
    grp_sums = summed[-1]
    basis = start_basis
    ortho = start_basis
    for round_index in range(2):
        factor = jnp.dot(total, basis, precision=highest)
        gram_part = jnp.dot(factor.T, factor, precision=highest)
        if round_index == 0:
            packed = lax.psum(jnp.concatenate([gram_part.reshape(-1), grp_sums]), "shard")
            gram = packed[: rank * rank].reshape(rank, rank)
            all_sums = packed[rank * rank :]
        else:
            gram = lax.psum(gram_part, "shard")
        lower_factor = jnp.linalg.cholesky(gram)
        ortho = jax.scipy.linalg.solve_triangular(lower_factor, factor.T, lower=True).T
        partial_basis = lax.dot_general(total, ortho, (((0,), (0,)), ((), ())), precision=highest)
        basis = lax.psum(partial_basis, "shard") / group_count
    approx = jnp.dot(ortho, basis.T, precision=highest)
    new_error = (corrected - approx)[None, :, :]
    new_momentum = momentum_decay * momentum + approx
    new_bias_momentum = momentum_decay * bias_momentum + all_sums / group_count
    new_weight = (weight.astype(jnp.float32) - learn_rate * new_momentum).astype(jnp.bfloat16)
    projected = jnp.dot(
        next_inputs,
        lax.all_gather(new_weight, "shard", axis=0, tiled=True),
        preferred_element_type=jnp.float32,
    )
    return (projected.astype(jnp.bfloat16), new_error, new_momentum, new_bias_momentum)


def solution(mesh):
    placed = (
        P(("grp", "shard"), None),
        P(("grp", "shard"), None),
        P("shard", None),
        P("grp", "shard", None),
        P("shard", None),
        P(),
        P(),
        P(("grp", "shard"), None),
    )
    return jax.shard_map(
        shards,
        mesh=mesh,
        in_specs=placed,
        out_specs=(P(("grp", "shard"), None), P("grp", "shard", None), P("shard", None), P()),
        check_vma=False,
    )
```

profile of v0, /device:TPU:1, one launch (start us, length us, event | category | flops | bytes accessed | tf_op | source)
XLA Modules:
  0.0 473.4 jit_solution(3598170805652788617)
XLA Ops:
  7.2 0.0 copy-start
  7.2 0.0 reduce-scatter.4.cloned.1.call-start
  7.2 1.4 copy-done
  8.6 6.3 %convolution_convert_fusion = bf16[1600,1600]{1,0:T(8,128)(2,1)} fusion(bf16[512,1600]{0,1:T(8,128)(2,1)S(1)} %copy-done, bf16[512,1600]{0,1:T(8,128)(2,1)} %param.12), kind=kOutput, calls=%fused_computation | convolution fusion | flops 2624000000 | bytes 8396800 | tf_op jit(solution)/shard_map/dot_general | solution.py:17
  14.9 0.0 copy-start.3
  14.9 0.0 reduce-scatter.4.cloned.1.call-update
  14.9 0.0 all-reduce.5.cloned.1.call-start
  15.0 1.4 copy-done.3
  16.4 0.3 convert_reduce_fusion
  16.7 48.7 %reduce-scatter.4.cloned.1.call-done = bf16[200,1600]{1,0:T(8,128)(2,1)} async-done(((bf16[1600,1600]{1,0:T(8,128)(2,1)}), bf16[200,1600]{1,0:T(8,128)(2,1)}) %reduce-scatter.4.cloned.1.call-update) | async-done | bytes 640016
  65.4 1.6 bitcast_add_fusion
  67.0 0.0 copy-start.2
  67.0 1.1 copy-done.2
  68.1 0.0 copy-start.4
  68.1 1.2 pad_maximum_fusion
  69.3 0.0 all-reduce.5.cloned.1.call-update
  69.3 0.0 all-reduce.7.cloned.1.call-start
  69.3 149.4 %all-reduce.5.cloned.1.call-done = f32[201,1600]{1,0:T(8,128)} async-done(((f32[201,1600]{1,0:T(8,128)}), f32[201,1600]{1,0:T(8,128)}) %all-reduce.5.cloned.1.call-update) | async-done | bytes 1286416 | tf_op jit(solution)/shard_map/psum | solution.py:26
  218.7 0.0 copy-done.4
  218.7 0.0 copy-start.1
  218.7 2.8 fusion.7
  221.5 0.2 fusion.31
  221.7 0.1 reshape.30
  221.7 0.0 copy-done.1
  221.8 25.7 %psum.36 = f32[2624]{0:T(1024)S(1)} all-reduce(f32[2624]{0:T(1024)S(1)} %pad_maximum_fusion.1), channel_id=1, replica_groups=mesh['grp'=32,'shard'=8] {'shard'}, use_global_device_ids=true, to_apply=%region_3.0 | all-reduce | flops 2624 | bytes 20992 | tf_op jit(solution)/shard_map/psum | solution.py:35
  247.5 0.1 reshape.31
  247.6 0.1 copy.18
  247.7 2.9 cholesky.44
  250.6 0.6 compare_reduce_fusion.1
  251.3 0.7 fusion.18
  251.9 2.4 custom-call.6
  254.4 0.2 fusion.16
  254.6 1.7 fusion.5
  256.3 0.0 all-reduce.7.cloned.1.call-update
  256.3 0.0 all-reduce.9.cloned.1.call-start
  256.4 60.6 %all-reduce.7.cloned.1.call-done = f32[1600,32]{0,1:T(8,128)} async-done(((f32[1600,32]{0,1:T(8,128)}), f32[1600,32]{0,1:T(8,128)}) %all-reduce.7.cloned.1.call-update) | async-done | bytes 204816 | tf_op jit(solution)/shard_map/psum | solution.py:43
  317.0 2.3 fusion.3
  319.2 0.2 fusion.32
  319.4 21.9 %psum.38 = f32[32,32]{0,1:T(8,128)S(1)} all-reduce(f32[32,32]{0,1:T(8,128)S(1)} %fusion.32), channel_id=1, replica_groups=mesh['grp'=32,'shard'=8] {'shard'}, use_global_device_ids=true, to_apply=%region_7.10 | all-reduce | flops 1024 | bytes 8192 | tf_op jit(solution)/shard_map/psum | solution.py:39
  341.3 0.1 copy.20
  341.4 2.9 cholesky.55
  344.4 0.6 compare_reduce_fusion
  345.0 0.7 fusion.19
  345.7 2.4 custom-call.7
  348.1 0.2 fusion.14
  348.3 1.7 fusion.1
  350.0 0.0 all-reduce.9.cloned.1.call-update
  350.0 0.0 copy-start.5
  350.0 0.0 all-gather.2.cloned.1.call-start
  350.1 64.9 %all-reduce.9.cloned.1.call-done = f32[1600,32]{0,1:T(8,128)} async-done(((f32[1600,32]{0,1:T(8,128)}), f32[1600,32]{0,1:T(8,128)}) %all-reduce.9.cloned.1.call-update) | async-done | bytes 204816 | tf_op jit(solution)/shard_map/psum | solution.py:43
  415.0 5.2 %subtract_convert_fusion = (bf16[200,1600]{1,0:T(8,128)(2,1)}, f32[200,1600]{1,0:T(8,128)}, f32[1,200,1600]{2,1,0:T(8,128)}) fusion(bf16[200,1600]{1,0:T(8,128)(2,1)} %param.13, f32[200,1600]{1,0:T(8,128)} %param.15, f32[200,1600]{1,0:T(8,128)} %copy-done.2, f32[32,200]{1,0:T(8,128)S(1)} %fusion.14, f32[1600,32]{0,1:T(8,128)} %all-reduce.9.cloned.1.call-done), kind=kOutput, calls=%fused_computation.7 | convolution fusion | flops 125171200 | bytes 6630400 | tf_op jit(solution)/shard_map/dot_general | solution.py:44
  420.2 0.0 all-gather.2.cloned.1.call-update
  420.2 0.0 copy-done.5
  420.2 0.6 fusion.26
  420.8 38.7 %all-gather.2.cloned.1.call-done = bf16[1600,1600]{1,0:T(8,128)(2,1)} async-done(((bf16[200,1600]{1,0:T(8,128)(2,1)}), bf16[1600,1600]{1,0:T(8,128)(2,1)}) %all-gather.2.cloned.1.call-update) | async-done | bytes 5120016 | tf_op jit(solution)/shard_map/all_gather | solution.py:51
  459.5 7.4 %fusion = bf16[512,1600]{0,1:T(8,128)(2,1)} fusion(bf16[1600,1600]{1,0:T(8,128)(2,1)} %all-gather.2.cloned.1.call-done, bf16[512,1600]{0,1:T(8,128)(2,1)} %param.18), kind=kOutput, calls=%fused_computation.3 | convolution fusion | flops 2622259200 | bytes 8396800 | tf_op jit(solution)/shard_map/dot_general | solution.py:49
  (8 shorter events, 0.1 us)
Async XLA Ops:
  7.2 1.4 copy-start
  7.2 58.2 %reduce-scatter.4.cloned.1.call-start = ((), (), s32[]{:S(2)}) async-start(), calls=%async_computation.5 | async-start | bytes 5990400
  14.9 1.4 copy-start.3
  14.9 203.7 %all-reduce.5.cloned.1.call-start = ((), (), s32[]{:S(2)}) async-start(), calls=%async_computation.1 | async-start | bytes 2768896 | tf_op jit(solution)/shard_map/psum | solution.py:26
  67.0 1.1 copy-start.2
  68.1 150.6 %copy-start.4 = (f32[1600,32]{0,1:T(8,128)S(1)}, f32[1600,32]{0,1:T(8,128)}, u32[]{:S(2)}) copy-start(f32[1600,32]{0,1:T(8,128)} %param.17) | copy-start | bytes 614404
  69.3 247.7 %all-reduce.7.cloned.1.call-start = ((), (), s32[]{:S(2)}) async-start(), calls=%async_computation.2 | async-start | bytes 425984 | tf_op jit(solution)/shard_map/psum | solution.py:43
  218.7 3.0 copy-start.1
  256.3 158.7 %all-reduce.9.cloned.1.call-start = ((), (), s32[]{:S(2)}) async-start(), calls=%async_computation.3 | async-start | bytes 425984 | tf_op jit(solution)/shard_map/psum | solution.py:43
  350.0 70.2 %copy-start.5 = (f32[1600]{0:T(1024)S(1)}, f32[1600]{0:T(1024)}, u32[]{:S(2)}) copy-start(f32[1600]{0:T(1024)} %param.16) | copy-start | bytes 19204
  350.0 109.5 %all-gather.2.cloned.1.call-start = ((), (), s32[]{:S(2)}) async-start(), calls=%async_computation.4 | async-start | bytes 5990400 | tf_op jit(solution)/shard_map/all_gather | solution.py:51
Sparse Core Ops, SparseCore 0:
  15.1 50.2 reduce-scatter.3
  69.4 149.1 all-reduce.4
  256.4 60.4 all-reduce.6
  350.1 64.7 all-reduce.8
  420.3 39.1 all-gather.1
where the time goes:
time: 474 us; the launch traced here: 473 us
  waiting for transfers between devices  362 us (76%)
  blocking collectives  47.7 us (10%)
  matrix products  28.1 us (6%)
  other arithmetic  17.1 us (4%)
  between operations  13.9 us (3%)
    psum x1, waiting for transfers between devices, shards(): lax.psum(jnp.concatenate([corrected, column_sums[None, :]], axis=0), 'grp')  149 us
    psum x2, waiting for transfers between devices, shards(): basis = lax.psum(partial_basis, 'shard') / group_count  125 us
    unnamed x6, waiting for transfers between devices  48.8 us
    all_gather x1, waiting for transfers between devices, shards(): lax.all_gather(new_weight, 'shard', axis=0, tiled=True)  38.7 us
    psum x1, blocking collectives, shards(): lax.psum(jnp.concatenate([gram_part.reshape(-1), grp_sums]), 'shard')  25.7 us
    psum x1, blocking collectives, shards(): gram = lax.psum(gram_part, 'shard')  21.9 us
  transfers between devices with their start and end apart: 5, of which 5 were waited for; matrix products, arithmetic and copies ran while one was open for 0% of the time, Pallas kernels for 0%

commit v1 on v0

--- a/solution.py
+++ b/solution.py
@@ -48,7 +48,9 @@
     new_weight = (weight.astype(jnp.float32) - learn_rate * new_momentum).astype(jnp.bfloat16)
     projected = jnp.dot(
         next_inputs,
-        lax.all_gather(new_weight, "shard", axis=0, tiled=True),
+        jnp.concatenate(
+            lax.all_to_all(jnp.stack([new_weight] * lax.axis_size("shard")), "shard", 0, 0), axis=0
+        ),
         preferred_element_type=jnp.float32,
     )
     return (projected.astype(jnp.bfloat16), new_error, new_momentum, new_bias_momentum)

time: 474 us -> 504 us (1.063)
  waiting for transfers between devices: 362 us -> 384 us
  starting transfers between devices: 0.21 us -> 6.17 us
    all_to_all x0 -> x1, waiting for transfers between devices: none -> 60.3 us  [shards(): lax.all_to_all(jnp.stack([new_weight] * lax.axis_size('shard')), 'shard',...]
    all_gather x1 -> x0, waiting for transfers between devices: 38.7 us -> none  [shards(): lax.all_gather(new_weight, 'shard', axis=0, tiled=True)]
    all_to_all x0 -> x1, starting transfers between devices: none -> 6 us  [shards(): lax.all_to_all(jnp.stack([new_weight] * lax.axis_size('shard')), 'shard',...]
    unnamed x6 -> x5, waiting for transfers between devices: 48.8 us -> 48.7 us
where the time goes in v1:
time: 504 us; the launch traced here: 503 us
  waiting for transfers between devices  384 us (76%)
  blocking collectives  47.7 us (9%)
  matrix products  27.9 us (6%)
  other arithmetic  17.1 us (3%)
  between operations  13.9 us (3%)
  local copies, waits for them, and re-layouts  6.86 us (1%)
  starting transfers between devices  6.17 us (1%)
    psum x1, waiting for transfers between devices, shards(): lax.psum(jnp.concatenate([corrected, column_sums[None, :]], axis=0), 'grp')  149 us
    psum x2, waiting for transfers between devices, shards(): basis = lax.psum(partial_basis, 'shard') / group_count  126 us
    all_to_all x1, waiting for transfers between devices, shards(): lax.all_to_all(jnp.stack([new_weight] * lax.axis_size('shard')), 'shard',...  60.3 us
    unnamed x5, waiting for transfers between devices  48.7 us
    psum x1, blocking collectives, shards(): lax.psum(jnp.concatenate([gram_part.reshape(-1), grp_sums]), 'shard')  25.7 us
    psum x1, blocking collectives, shards(): gram = lax.psum(gram_part, 'shard')  21.9 us
  transfers between devices with their start and end apart: 5, of which 5 were waited for; matrix products, arithmetic and copies ran while one was open for 0% of the time, Pallas kernels for 0%

profile of v1, /device:TPU:1, one launch (start us, length us, event | category | flops | bytes accessed | tf_op | source)
XLA Modules:
  0.0 503.2 jit_solution(12014447005722340320)
XLA Ops:
  7.2 0.0 copy-start
  7.2 0.0 reduce-scatter.4.cloned.1.call-start
  7.2 1.4 copy-done
  8.6 6.3 %convolution_convert_fusion = bf16[1600,1600]{1,0:T(8,128)(2,1)} fusion(bf16[512,1600]{0,1:T(8,128)(2,1)S(1)} %copy-done, bf16[512,1600]{0,1:T(8,128)(2,1)} %param.12), kind=kOutput, calls=%fused_computation | convolution fusion | flops 2624000000 | bytes 8396800 | tf_op jit(solution)/shard_map/dot_general | solution.py:17
  14.9 0.0 copy-start.3
  14.9 0.0 reduce-scatter.4.cloned.1.call-update
  15.0 0.0 all-reduce.5.cloned.1.call-start
  15.0 1.4 copy-done.3
  16.4 0.3 convert_reduce_fusion
  16.7 48.6 %reduce-scatter.4.cloned.1.call-done = bf16[200,1600]{1,0:T(8,128)(2,1)} async-done(((bf16[1600,1600]{1,0:T(8,128)(2,1)}), bf16[200,1600]{1,0:T(8,128)(2,1)}) %reduce-scatter.4.cloned.1.call-update) | async-done | bytes 640016
  65.3 1.6 bitcast_add_fusion
  66.9 0.0 copy-start.2
  66.9 1.1 copy-done.2
  68.0 0.0 copy-start.4
  68.0 1.2 pad_maximum_fusion
  69.1 0.0 all-reduce.5.cloned.1.call-update
  69.2 0.0 all-reduce.7.cloned.1.call-start
  69.2 149.1 %all-reduce.5.cloned.1.call-done = f32[201,1600]{1,0:T(8,128)} async-done(((f32[201,1600]{1,0:T(8,128)}), f32[201,1600]{1,0:T(8,128)}) %all-reduce.5.cloned.1.call-update) | async-done | bytes 1286416 | tf_op jit(solution)/shard_map/psum | solution.py:26
  218.4 0.0 copy-done.4
  218.4 0.0 copy-start.1
  218.4 2.8 fusion.7
  221.2 0.2 fusion.31
  221.3 0.1 reshape.35
  221.4 0.0 copy-done.1
  221.4 25.7 %psum.36 = f32[2624]{0:T(1024)S(1)} all-reduce(f32[2624]{0:T(1024)S(1)} %pad_maximum_fusion.1), channel_id=1, replica_groups=mesh['grp'=32,'shard'=8] {'shard'}, use_global_device_ids=true, to_apply=%region_3.0 | all-reduce | flops 2624 | bytes 20992 | tf_op jit(solution)/shard_map/psum | solution.py:35
  247.2 0.1 reshape.36
  247.3 0.1 copy.18
  247.3 2.9 cholesky.44
  250.3 0.6 compare_reduce_fusion.1
  250.9 0.7 fusion.18
  251.6 2.4 custom-call.6
  254.0 0.2 fusion.16
  254.3 1.7 fusion.5
  256.0 0.0 all-reduce.7.cloned.1.call-update
  256.0 0.0 all-reduce.9.cloned.1.call-start
  256.0 60.6 %all-reduce.7.cloned.1.call-done = f32[1600,32]{0,1:T(8,128)} async-done(((f32[1600,32]{0,1:T(8,128)}), f32[1600,32]{0,1:T(8,128)}) %all-reduce.7.cloned.1.call-update) | async-done | bytes 204816 | tf_op jit(solution)/shard_map/psum | solution.py:43
  316.6 2.3 fusion.3
  318.9 0.2 fusion.32
  319.1 21.9 %psum.38 = f32[32,32]{0,1:T(8,128)S(1)} all-reduce(f32[32,32]{0,1:T(8,128)S(1)} %fusion.32), channel_id=1, replica_groups=mesh['grp'=32,'shard'=8] {'shard'}, use_global_device_ids=true, to_apply=%region_7.10 | all-reduce | flops 1024 | bytes 8192 | tf_op jit(solution)/shard_map/psum | solution.py:39
  341.0 0.1 copy.20
  341.1 2.9 cholesky.55
  344.0 0.6 compare_reduce_fusion
  344.7 0.7 fusion.19
  345.3 2.4 custom-call.7
  347.8 0.2 fusion.14
  348.0 1.7 fusion.1
  349.7 0.0 all-reduce.9.cloned.1.call-update
  349.7 65.0 %all-reduce.9.cloned.1.call-done = f32[1600,32]{0,1:T(8,128)} async-done(((f32[1600,32]{0,1:T(8,128)}), f32[1600,32]{0,1:T(8,128)}) %all-reduce.9.cloned.1.call-update) | async-done | bytes 204816 | tf_op jit(solution)/shard_map/psum | solution.py:43
  414.6 5.0 subtract_convert_fusion
  419.6 2.7 stack.2
  422.3 0.0 copy-start.5
  422.3 6.0 %all-to-all-start = ((bf16[8,200,1600]{2,1,0:T(8,128)(2,1)}), bf16[8,200,1600]{2,1,0:T(8,128)(2,1)}, u32[]{:S(2)}, u32[]{:S(2)}) async-start(bf16[8,200,1600]{2,1,0:T(8,128)(2,1)} %stack.2), calls=%async_computation | async-start | bytes 10649600 | tf_op jit(solution)/shard_map/all_to_all | solution.py:52
  428.4 0.0 copy-done.5
  428.4 0.6 fusion.26
  429.0 60.3 %all-to-all-done = bf16[8,200,1600]{2,1,0:T(8,128)(2,1)} async-done(((bf16[8,200,1600]{2,1,0:T(8,128)(2,1)}), bf16[8,200,1600]{2,1,0:T(8,128)(2,1)}, u32[]{:S(2)}, u32[]{:S(2)}) %all-to-all-start) | async-done | bytes 5120032 | tf_op jit(solution)/shard_map/all_to_all | solution.py:52
  489.3 7.4 %fusion = bf16[512,1600]{0,1:T(8,128)(2,1)} fusion(bf16[1600,1600]{1,0:T(8,128)(2,1)} %bitcast.9, bf16[512,1600]{0,1:T(8,128)(2,1)} %param.18), kind=kOutput, calls=%fused_computation.3 | convolution fusion | flops 2622259200 | bytes 8396800 | tf_op jit(solution)/shard_map/dot_general | solution.py:49
  (8 shorter events, 0.1 us)
Async XLA Ops:
  7.2 1.4 copy-start
  7.2 58.1 %reduce-scatter.4.cloned.1.call-start = ((), (), s32[]{:S(2)}) async-start(), calls=%async_computation.5 | async-start | bytes 5990400
  14.9 1.4 copy-start.3
  15.0 203.4 %all-reduce.5.cloned.1.call-start = ((), (), s32[]{:S(2)}) async-start(), calls=%async_computation.2 | async-start | bytes 2768896 | tf_op jit(solution)/shard_map/psum | solution.py:26
  66.9 1.1 copy-start.2
  68.0 150.4 %copy-start.4 = (f32[1600,32]{0,1:T(8,128)S(1)}, f32[1600,32]{0,1:T(8,128)}, u32[]{:S(2)}) copy-start(f32[1600,32]{0,1:T(8,128)} %param.17) | copy-start | bytes 614404
  69.2 247.4 %all-reduce.7.cloned.1.call-start = ((), (), s32[]{:S(2)}) async-start(), calls=%async_computation.3 | async-start | bytes 425984 | tf_op jit(solution)/shard_map/psum | solution.py:43
  218.4 3.0 copy-start.1
  256.0 158.7 %all-reduce.9.cloned.1.call-start = ((), (), s32[]{:S(2)}) async-start(), calls=%async_computation.4 | async-start | bytes 425984 | tf_op jit(solution)/shard_map/psum | solution.py:43
  422.3 6.0 %copy-start.5 = (f32[1600]{0:T(1024)S(1)}, f32[1600]{0:T(1024)}, u32[]{:S(2)}) copy-start(f32[1600]{0:T(1024)} %param.16) | copy-start | bytes 19204
  422.3 66.9 %all-to-all-start = ((bf16[8,200,1600]{2,1,0:T(8,128)(2,1)}), bf16[8,200,1600]{2,1,0:T(8,128)(2,1)}, u32[]{:S(2)}, u32[]{:S(2)}) async-start(bf16[8,200,1600]{2,1,0:T(8,128)(2,1)} %stack.2), calls=%async_computation | async-start | bytes 10649600 | tf_op jit(solution)/shard_map/all_to_all | solution.py:52
Sparse Core Ops, SparseCore 0:
  15.1 50.1 reduce-scatter.3
  69.3 148.9 all-reduce.4
  256.1 60.4 all-reduce.6
  349.8 64.7 all-reduce.8
